TPU v7x, 512 devices: a whole 4x4x16 slice. The times are simulated.
512 devices in a mesh: context: 64 (over x, z), tensor: 8 (over y, core).
Axes of the slice: x: 4, y: 4, z: 16, core: 2. Of those that a mesh axis runs over, the one named last changes fastest.
Arguments:
- inputs: bfloat16 [8192, 8192], P('context', 'tensor'), may hold values from -0.8984375 to 0.8984375
- grads: bfloat16 [8192, 8192], P('context', 'tensor'), may hold values from -0.8984375 to 0.8984375
- step_size: float32 [128, 8192], P('tensor', 'context'), may hold values from 0.25 to 4
- decay_rate: float32 [128], P('tensor'), may hold values from 0 to 1, as said below
- skip_gain: float32 [128], P('tensor'), may hold values from 0.5 to 1.5
- b_rows: bfloat16 [8192, 128], P(('context', 'tensor')), may hold values from -0.59765625 to 0.59765625
- c_rows: bfloat16 [8192, 128], P(('context', 'tensor')), may hold values from -0.59765625 to 0.59765625
- doc_lengths: int32 [64], replicated, may hold values from 1 to 1536, 8192 in all
Outputs:
- grad_x: float32 [8192, 8192], P('context', 'tensor')
- grad_step: float32 [128, 8192], P('tensor', 'context')
- grad_b: float32 [8192, 128], P(('context', 'tensor'))
- grad_c: float32 [8192, 128], P(('context', 'tensor'))
Inputs may be any that keep to these rules, and one draw needn't show every extreme that they name: doc_lengths sum to 8192; the longest document has exactly 1536 tokens. `decay_rate`: decay rates are positive.
All inputs are finite; a program needn't handle non-finite values.
Results may differ from a plain program's by a relative error of at most 0.0005.
Values may be sent and summed in bfloat16 or wider, within the bound.
No kernel may reach another device: no remote copies, remote signals or barrier semaphores. Data moves between devices by JAX's collectives and lax.ppermute only.
A program may use at most 192 MiB of HBM per device.

v0:
```python
import jax
import jax.numpy as jnp
from jax import lax
from jax.sharding import PartitionSpec as P

HIGH = lax.Precision.HIGHEST


def from_behind(x, axis, by):
    peers = lax.axis_size(axis)
    pairs = [(i, i + by) for i in range(peers) if 0 <= i + by < peers]
    return lax.ppermute(x, axis, pairs)


def local(inputs, grads, step_size, decay_rate, skip_gain, b_rows, c_rows, doc_lengths):
    length = inputs.shape[0]
    heads = step_size.shape[0]
    width = inputs.shape[1] // heads
    rows = lax.all_gather(jnp.stack([b_rows, c_rows]), "tensor", axis=1, tiled=True)
    b_bf, c_bf = (rows[0], rows[1])
    bmat = b_bf.astype(jnp.float32)
    cmat = c_bf.astype(jnp.float32)
    xs = inputs.astype(jnp.float32).reshape(length, heads, width).transpose(1, 0, 2)
    dys = grads.astype(jnp.float32).reshape(length, heads, width).transpose(1, 0, 2)
    offset = lax.axis_index("context") * length
    ends = jnp.cumsum(doc_lengths)
    starts = ends - doc_lengths
    position = offset + jnp.arange(length, dtype=jnp.int32)
    seg = jnp.sum(
        ((starts[None, :] >= offset) & (starts[None, :] <= position[:, None])).astype(jnp.int32),
        axis=1,
    )
    rate = decay_rate[:, None]
    logc = jnp.cumsum(-step_size * rate, axis=1)
    enter = jnp.exp(logc) * (seg == 0).astype(jnp.float32)[None, :]
    leave = jnp.exp(logc[:, -1:] - logc) * (seg == seg[-1]).astype(jnp.float32)[None, :]
    total = enter[:, -1][:, None, None]
    moved = step_size[:, :, None] * xs
    left_u = leave[:, :, None] * moved
    enter_dy = enter[:, :, None] * dys
    local_state = jnp.einsum("hlp,ln->hpn", left_u, bmat, precision=HIGH)
    local_adj = jnp.einsum("hlp,ln->hpn", enter_dy, cmat, precision=HIGH)
    turns = 3 * lax.axis_size("context") // 16
    inc_state = jnp.zeros_like(local_state)
    inc_adj = jnp.zeros_like(local_adj)
    for _ in range(turns):
        send_state, send_adj = lax.optimization_barrier(
            (local_state + total * inc_state, local_adj + total * inc_adj)
        )
        inc_state, inc_adj = lax.optimization_barrier(
            (from_behind(send_state, "context", 1), from_behind(send_adj, "context", -1))
        )
    s_in, g_in = (inc_state, inc_adj)
    index = jnp.arange(length)
    keep = (index[:, None] >= index[None, :]) & (seg[:, None] == seg[None, :])
    weights = jnp.exp(jnp.where(keep[None], logc[:, :, None] - logc[:, None, :], -1e30))
    scores = jnp.dot(c_bf, b_bf.T, preferred_element_type=jnp.float32)
    mixed = weights * scores[None]
    core_loc = jnp.einsum("hij,hip->hjp", mixed, dys, precision=HIGH)
    pairs = jnp.einsum("hip,hjp->hij", dys, moved, precision=HIGH)
    paired = mixed * pairs
    col_total = jnp.sum(paired, axis=1)
    row_total = jnp.sum(paired, axis=2)
    inner = jnp.cumsum(col_total, axis=1) - (jnp.cumsum(row_total, axis=1) - row_total)
    weighted = jnp.sum(weights * pairs, axis=0)
    gb_loc = jnp.dot(weighted.T, cmat, precision=HIGH)
    gc_loc = jnp.dot(weighted, bmat, precision=HIGH)
    b_adj = jnp.einsum("ln,hpn->hlp", bmat, g_in, precision=HIGH)
    c_state = jnp.einsum("ln,hpn->hlp", cmat, s_in, precision=HIGH)
    core = core_loc + leave[:, :, None] * b_adj
    gx = step_size[:, :, None] * core + skip_gain[:, None, None] * dys
    along = jnp.sum(xs * core, axis=2)
    from_state = enter * jnp.einsum(
        "hij,hi->hj", weights, jnp.sum(dys * c_state, axis=2), precision=HIGH
    )
    from_adj = leave * jnp.einsum(
        "hij,hj->hi", weights, jnp.sum(moved * b_adj, axis=2), precision=HIGH
    )
    both = leave * enter * jnp.sum(g_in * s_in, axis=(1, 2))[:, None]
    grad_step = along * (1.0 + rate * step_size) - rate * (inner + from_state + from_adj + both)
    gb = gb_loc + jnp.einsum("hlp,hpn->ln", left_u, g_in, precision=HIGH)
    gc = gc_loc + jnp.einsum("hlp,hpn->ln", enter_dy, s_in, precision=HIGH)
    grad_x = gx.transpose(1, 0, 2).reshape(length, heads * width)
    grad_bc = lax.psum_scatter(jnp.stack([gb, gc]), "tensor", scatter_dimension=1, tiled=True)
    return (grad_x, grad_step, grad_bc[0], grad_bc[1])


def solution(mesh):
    in_specs = (
        P("context", "tensor"),
        P("context", "tensor"),
        P("tensor", "context"),
        P("tensor"),
        P("tensor"),
        P(("context", "tensor"), None),
        P(("context", "tensor"), None),
        P(),
    )
    out_specs = (
        P("context", "tensor"),
        P("tensor", "context"),
        P(("context", "tensor"), None),
        P(("context", "tensor"), None),
    )
    return jax.shard_map(local, mesh=mesh, in_specs=in_specs, out_specs=out_specs, check_vma=False)
```

profile of v0, /device:TPU:2, one launch (start us, length us, event | category | flops | bytes accessed | tf_op | source)
XLA Modules:
  0.0 278.4 jit_solution(14510431676233515382)
XLA Ops:
  10.7 13.3 %all_gather.3 = bf16[2,128,128]{2,1,0:T(8,128)(2,1)S(1)} all-gather(bf16[2,16,128]{2,1,0:T(8,128)(2,1)S(1)} %pad_maximum_fusion.1), channel_id=1, replica_groups=mesh['context'=64,'tensor'=8] {'tensor'}, dimensions={1}, use_global_device_ids=true | all-gather | bytes 73728 | tf_op jit(solution)/shard_map/all_gather | solution.py:19
  26.3 3.8 %collective-permute-start = (f32[16,64,128]{2,1,0:T(8,128)S(1)}, f32[16,64,128]{2,1,0:T(8,128)S(1)}, u32[]{:S(2)}, u32[]{:S(2)}) collective-permute-start(f32[16,64,128]{2,1,0:T(8,128)S(1)} %get-tuple-element.52), channel_id=1, source_target_pairs={{0,8},{8,16},{16,24},{24,32},{32,40},{40,48},{48,56},{56,64},{64,7... | collective-permute-start | bytes 1572872 | tf_op jit(solution)/shard_map/ppermute | solution.py:12
  30.2 9.5 %collective-permute-start.1 = (f32[16,64,128]{2,1,0:T(8,128)S(1)}, f32[16,64,128]{2,1,0:T(8,128)S(1)}, u32[]{:S(2)}, u32[]{:S(2)}) collective-permute-start(f32[16,64,128]{2,1,0:T(8,128)S(1)} %get-tuple-element.53), channel_id=1, source_target_pairs={{8,0},{16,8},{24,16},{32,24},{40,32},{48,40},{56,48},{64,56},{72,6... | collective-permute-start | bytes 1572872 | tf_op jit(solution)/shard_map/ppermute | solution.py:12
  39.6 10.5 %collective-permute-done = f32[16,64,128]{2,1,0:T(8,128)S(1)} collective-permute-done((f32[16,64,128]{2,1,0:T(8,128)S(1)}, f32[16,64,128]{2,1,0:T(8,128)S(1)}, u32[]{:S(2)}, u32[]{:S(2)}) %collective-permute-start) | collective-permute-done | bytes 524320 | tf_op jit(solution)/shard_map/ppermute | solution.py:12
  51.5 1.9 collective-permute-start.2
  53.4 6.5 %collective-permute-start.3 = (f32[16,64,128]{2,1,0:T(8,128)S(1)}, f32[16,64,128]{2,1,0:T(8,128)S(1)}, u32[]{:S(2)}, u32[]{:S(2)}) collective-permute-start(f32[16,64,128]{2,1,0:T(8,128)S(1)} %get-tuple-element.57), channel_id=1, source_target_pairs={{8,0},{16,8},{24,16},{32,24},{40,32},{48,40},{56,48},{64,56},{72,6... | collective-permute-start | bytes 1572872 | tf_op jit(solution)/shard_map/ppermute | solution.py:12
  59.9 9.7 %collective-permute-done.2 = f32[16,64,128]{2,1,0:T(8,128)S(1)} collective-permute-done((f32[16,64,128]{2,1,0:T(8,128)S(1)}, f32[16,64,128]{2,1,0:T(8,128)S(1)}, u32[]{:S(2)}, u32[]{:S(2)}) %collective-permute-start.2) | collective-permute-done | bytes 524320 | tf_op jit(solution)/shard_map/ppermute | solution.py:12
  70.9 1.9 collective-permute-start.4
  72.8 6.5 %collective-permute-start.5 = (f32[16,64,128]{2,1,0:T(8,128)S(1)}, f32[16,64,128]{2,1,0:T(8,128)S(1)}, u32[]{:S(2)}, u32[]{:S(2)}) collective-permute-start(f32[16,64,128]{2,1,0:T(8,128)S(1)} %get-tuple-element.61), channel_id=1, source_target_pairs={{8,0},{16,8},{24,16},{32,24},{40,32},{48,40},{56,48},{64,56},{72,6... | collective-permute-start | bytes 1572872 | tf_op jit(solution)/shard_map/ppermute | solution.py:12
  79.3 8.7 %collective-permute-done.4 = f32[16,64,128]{2,1,0:T(8,128)S(1)} collective-permute-done((f32[16,64,128]{2,1,0:T(8,128)S(1)}, f32[16,64,128]{2,1,0:T(8,128)S(1)}, u32[]{:S(2)}, u32[]{:S(2)}) %collective-permute-start.4) | collective-permute-done | bytes 524320 | tf_op jit(solution)/shard_map/ppermute | solution.py:12
  89.4 1.9 collective-permute-start.6
  91.4 6.5 %collective-permute-start.7 = (f32[16,64,128]{2,1,0:T(8,128)S(1)}, f32[16,64,128]{2,1,0:T(8,128)S(1)}, u32[]{:S(2)}, u32[]{:S(2)}) collective-permute-start(f32[16,64,128]{2,1,0:T(8,128)S(1)} %get-tuple-element.65), channel_id=1, source_target_pairs={{8,0},{16,8},{24,16},{32,24},{40,32},{48,40},{56,48},{64,56},{72,6... | collective-permute-start | bytes 1572872 | tf_op jit(solution)/shard_map/ppermute | solution.py:12
  97.9 7.8 %collective-permute-done.6 = f32[16,64,128]{2,1,0:T(8,128)S(1)} collective-permute-done((f32[16,64,128]{2,1,0:T(8,128)S(1)}, f32[16,64,128]{2,1,0:T(8,128)S(1)}, u32[]{:S(2)}, u32[]{:S(2)}) %collective-permute-start.6) | collective-permute-done | bytes 524320 | tf_op jit(solution)/shard_map/ppermute | solution.py:12
  107.0 1.9 collective-permute-start.8
  109.0 6.5 %collective-permute-start.9 = (f32[16,64,128]{2,1,0:T(8,128)S(1)}, f32[16,64,128]{2,1,0:T(8,128)S(1)}, u32[]{:S(2)}, u32[]{:S(2)}) collective-permute-start(f32[16,64,128]{2,1,0:T(8,128)S(1)} %get-tuple-element.69), channel_id=1, source_target_pairs={{8,0},{16,8},{24,16},{32,24},{40,32},{48,40},{56,48},{64,56},{72,6... | collective-permute-start | bytes 1572872 | tf_op jit(solution)/shard_map/ppermute | solution.py:12
  115.5 6.9 %collective-permute-done.8 = f32[16,64,128]{2,1,0:T(8,128)S(1)} collective-permute-done((f32[16,64,128]{2,1,0:T(8,128)S(1)}, f32[16,64,128]{2,1,0:T(8,128)S(1)}, u32[]{:S(2)}, u32[]{:S(2)}) %collective-permute-start.8) | collective-permute-done | bytes 524320 | tf_op jit(solution)/shard_map/ppermute | solution.py:12
  123.7 1.9 collective-permute-start.10
  125.7 6.5 %collective-permute-start.11 = (f32[16,64,128]{2,1,0:T(8,128)S(1)}, f32[16,64,128]{2,1,0:T(8,128)S(1)}, u32[]{:S(2)}, u32[]{:S(2)}) collective-permute-start(f32[16,64,128]{2,1,0:T(8,128)S(1)} %get-tuple-element.73), channel_id=1, source_target_pairs={{8,0},{16,8},{24,16},{32,24},{40,32},{48,40},{56,48},{64,56},{72,6... | collective-permute-start | bytes 1572872 | tf_op jit(solution)/shard_map/ppermute | solution.py:12
  132.2 6.0 %collective-permute-done.10 = f32[16,64,128]{2,1,0:T(8,128)S(1)} collective-permute-done((f32[16,64,128]{2,1,0:T(8,128)S(1)}, f32[16,64,128]{2,1,0:T(8,128)S(1)}, u32[]{:S(2)}, u32[]{:S(2)}) %collective-permute-start.10) | collective-permute-done | bytes 524320 | tf_op jit(solution)/shard_map/ppermute | solution.py:12
  139.5 1.9 collective-permute-start.12
  141.4 6.5 %collective-permute-start.13 = (f32[16,64,128]{2,1,0:T(8,128)S(1)}, f32[16,64,128]{2,1,0:T(8,128)S(1)}, u32[]{:S(2)}, u32[]{:S(2)}) collective-permute-start(f32[16,64,128]{2,1,0:T(8,128)S(1)} %get-tuple-element.77), channel_id=1, source_target_pairs={{8,0},{16,8},{24,16},{32,24},{40,32},{48,40},{56,48},{64,56},{72,6... | collective-permute-start | bytes 1572872 | tf_op jit(solution)/shard_map/ppermute | solution.py:12
  147.9 5.2 %collective-permute-done.12 = f32[16,64,128]{2,1,0:T(8,128)S(1)} collective-permute-done((f32[16,64,128]{2,1,0:T(8,128)S(1)}, f32[16,64,128]{2,1,0:T(8,128)S(1)}, u32[]{:S(2)}, u32[]{:S(2)}) %collective-permute-start.12) | collective-permute-done | bytes 524320 | tf_op jit(solution)/shard_map/ppermute | solution.py:12
  153.1 1.5 collective-permute-done.13
  154.8 1.9 collective-permute-start.14
  156.7 6.5 %collective-permute-start.15 = (f32[16,64,128]{2,1,0:T(8,128)S(1)}, f32[16,64,128]{2,1,0:T(8,128)S(1)}, u32[]{:S(2)}, u32[]{:S(2)}) collective-permute-start(f32[16,64,128]{2,1,0:T(8,128)S(1)} %get-tuple-element.81), channel_id=1, source_target_pairs={{8,0},{16,8},{24,16},{32,24},{40,32},{48,40},{56,48},{64,56},{72,6... | collective-permute-start | bytes 1572872 | tf_op jit(solution)/shard_map/ppermute | solution.py:12
  163.2 5.2 %collective-permute-done.14 = f32[16,64,128]{2,1,0:T(8,128)S(1)} collective-permute-done((f32[16,64,128]{2,1,0:T(8,128)S(1)}, f32[16,64,128]{2,1,0:T(8,128)S(1)}, u32[]{:S(2)}, u32[]{:S(2)}) %collective-permute-start.14) | collective-permute-done | bytes 524320 | tf_op jit(solution)/shard_map/ppermute | solution.py:12
  168.4 1.5 collective-permute-done.15
  170.1 1.9 collective-permute-start.16
  172.0 6.5 %collective-permute-start.17 = (f32[16,64,128]{2,1,0:T(8,128)S(1)}, f32[16,64,128]{2,1,0:T(8,128)S(1)}, u32[]{:S(2)}, u32[]{:S(2)}) collective-permute-start(f32[16,64,128]{2,1,0:T(8,128)S(1)} %get-tuple-element.85), channel_id=1, source_target_pairs={{8,0},{16,8},{24,16},{32,24},{40,32},{48,40},{56,48},{64,56},{72,6... | collective-permute-start | bytes 1572872 | tf_op jit(solution)/shard_map/ppermute | solution.py:12
  178.5 5.2 %collective-permute-done.16 = f32[16,64,128]{2,1,0:T(8,128)S(1)} collective-permute-done((f32[16,64,128]{2,1,0:T(8,128)S(1)}, f32[16,64,128]{2,1,0:T(8,128)S(1)}, u32[]{:S(2)}, u32[]{:S(2)}) %collective-permute-start.16) | collective-permute-done | bytes 524320 | tf_op jit(solution)/shard_map/ppermute | solution.py:12
  183.7 1.5 collective-permute-done.17
  185.3 1.9 collective-permute-start.18
  187.3 6.5 %collective-permute-start.19 = (f32[16,64,128]{2,1,0:T(8,128)S(1)}, f32[16,64,128]{2,1,0:T(8,128)S(1)}, u32[]{:S(2)}, u32[]{:S(2)}) collective-permute-start(f32[16,64,128]{2,1,0:T(8,128)S(1)} %get-tuple-element.89), channel_id=1, source_target_pairs={{8,0},{16,8},{24,16},{32,24},{40,32},{48,40},{56,48},{64,56},{72,6... | collective-permute-start | bytes 1572872 | tf_op jit(solution)/shard_map/ppermute | solution.py:12
  193.8 5.9 %collective-permute-done.18 = f32[16,64,128]{2,1,0:T(8,128)S(1)} collective-permute-done((f32[16,64,128]{2,1,0:T(8,128)S(1)}, f32[16,64,128]{2,1,0:T(8,128)S(1)}, u32[]{:S(2)}, u32[]{:S(2)}) %collective-permute-start.18) | collective-permute-done | bytes 524320 | tf_op jit(solution)/shard_map/ppermute | solution.py:12
  199.6 1.7 collective-permute-done.19
  201.6 1.9 collective-permute-start.20
  203.5 6.5 %collective-permute-start.21 = (f32[16,64,128]{2,1,0:T(8,128)S(1)}, f32[16,64,128]{2,1,0:T(8,128)S(1)}, u32[]{:S(2)}, u32[]{:S(2)}) collective-permute-start(f32[16,64,128]{2,1,0:T(8,128)S(1)} %get-tuple-element.93), channel_id=1, source_target_pairs={{8,0},{16,8},{24,16},{32,24},{40,32},{48,40},{56,48},{64,56},{72,6... | collective-permute-start | bytes 1572872 | tf_op jit(solution)/shard_map/ppermute | solution.py:12
  210.7 1.5 fusion.12
  212.2 4.7 %collective-permute-done.20 = f32[16,64,128]{2,1,0:T(8,128)S(1)} collective-permute-done((f32[16,64,128]{2,1,0:T(8,128)S(1)}, f32[16,64,128]{2,1,0:T(8,128)S(1)}, u32[]{:S(2)}, u32[]{:S(2)}) %collective-permute-start.20) | collective-permute-done | bytes 524320 | tf_op jit(solution)/shard_map/ppermute | solution.py:12
  216.9 1.7 collective-permute-done.21
  218.8 2.1 collective-permute-start.22
  221.0 6.5 %collective-permute-start.23 = (f32[16,64,128]{2,1,0:T(8,128)S(1)}, f32[16,64,128]{2,1,0:T(8,128)S(1)}, u32[]{:S(2)}, u32[]{:S(2)}) collective-permute-start(f32[16,64,128]{2,1,0:T(8,128)S(1)} %get-tuple-element.97), channel_id=1, source_target_pairs={{8,0},{16,8},{24,16},{32,24},{40,32},{48,40},{56,48},{64,56},{72,6... | collective-permute-start | bytes 1572872 | tf_op jit(solution)/shard_map/ppermute | solution.py:12
  230.3 1.3 fusion.10
  232.5 1.5 collective-permute-done.23
  238.9 1.2 fusion.6
  240.0 1.9 fusion.7
  244.5 25.7 %reduce-scatter.2.cloned.1.call-done = f32[2,16,128]{2,1,0:T(8,128)} async-done(((f32[2,128,128]{2,1,0:T(8,128)}), f32[2,16,128]{2,1,0:T(8,128)}) %reduce-scatter.2.cloned.1.call-update) | async-done | bytes 16400 | tf_op jit(solution)/shard_map/reduce_scatter | solution.py:84
  270.2 1.3 slice_bitcast_fusion
  (100 shorter events, 26.4 us)
Async XLA Ops:
  7.2 263.0 %reduce-scatter.2.cloned.1.call-start = ((), (), s32[]{:S(2)}) async-start(), calls=%async_computation.1 | async-start | bytes 147456 | tf_op jit(solution)/shard_map/reduce_scatter | solution.py:84
  7.2 0.7 copy-start.19
  8.2 1.4 copy-start
  8.9 0.7 copy-start.20
  10.0 200.3 %copy-start.5 = (f32[16,128]{1,0:T(8,128)}, f32[16,128]{1,0:T(8,128)S(1)}, u32[]{:S(2)}) copy-start(f32[16,128]{1,0:T(8,128)S(1)} %reduce_window_sum.30) | copy-start | bytes 24580
  10.0 0.7 copy-start.17
  10.0 0.7 copy-start.18
  23.9 1.4 copy-start.1
  25.1 0.8 copy-start.2
  26.3 23.8 %collective-permute-start = (f32[16,64,128]{2,1,0:T(8,128)S(1)}, f32[16,64,128]{2,1,0:T(8,128)S(1)}, u32[]{:S(2)}, u32[]{:S(2)}) collective-permute-start(f32[16,64,128]{2,1,0:T(8,128)S(1)} %get-tuple-element.52), channel_id=1, source_target_pairs={{0,8},{8,16},{16,24},{24,32},{32,40},{40,48},{48,56},{56,64},{64,7... | collective-permute-start | bytes 1572872 | tf_op jit(solution)/shard_map/ppermute | solution.py:12
  30.2 21.1 %collective-permute-start.1 = (f32[16,64,128]{2,1,0:T(8,128)S(1)}, f32[16,64,128]{2,1,0:T(8,128)S(1)}, u32[]{:S(2)}, u32[]{:S(2)}) collective-permute-start(f32[16,64,128]{2,1,0:T(8,128)S(1)} %get-tuple-element.53), channel_id=1, source_target_pairs={{8,0},{16,8},{24,16},{32,24},{40,32},{48,40},{56,48},{64,56},{72,6... | collective-permute-start | bytes 1572872 | tf_op jit(solution)/shard_map/ppermute | solution.py:12
  51.5 18.1 %collective-permute-start.2 = (f32[16,64,128]{2,1,0:T(8,128)S(1)}, f32[16,64,128]{2,1,0:T(8,128)S(1)}, u32[]{:S(2)}, u32[]{:S(2)}) collective-permute-start(f32[16,64,128]{2,1,0:T(8,128)S(1)} %get-tuple-element.56), channel_id=1, source_target_pairs={{0,8},{8,16},{16,24},{24,32},{32,40},{40,48},{48,56},{56,64},{64,7... | collective-permute-start | bytes 1572872 | tf_op jit(solution)/shard_map/ppermute | solution.py:12
  53.4 17.3 %collective-permute-start.3 = (f32[16,64,128]{2,1,0:T(8,128)S(1)}, f32[16,64,128]{2,1,0:T(8,128)S(1)}, u32[]{:S(2)}, u32[]{:S(2)}) collective-permute-start(f32[16,64,128]{2,1,0:T(8,128)S(1)} %get-tuple-element.57), channel_id=1, source_target_pairs={{8,0},{16,8},{24,16},{32,24},{40,32},{48,40},{56,48},{64,56},{72,6... | collective-permute-start | bytes 1572872 | tf_op jit(solution)/shard_map/ppermute | solution.py:12
  70.9 17.2 %collective-permute-start.4 = (f32[16,64,128]{2,1,0:T(8,128)S(1)}, f32[16,64,128]{2,1,0:T(8,128)S(1)}, u32[]{:S(2)}, u32[]{:S(2)}) collective-permute-start(f32[16,64,128]{2,1,0:T(8,128)S(1)} %get-tuple-element.60), channel_id=1, source_target_pairs={{0,8},{8,16},{16,24},{24,32},{32,40},{40,48},{48,56},{56,64},{64,7... | collective-permute-start | bytes 1572872 | tf_op jit(solution)/shard_map/ppermute | solution.py:12
  72.8 16.4 %collective-permute-start.5 = (f32[16,64,128]{2,1,0:T(8,128)S(1)}, f32[16,64,128]{2,1,0:T(8,128)S(1)}, u32[]{:S(2)}, u32[]{:S(2)}) collective-permute-start(f32[16,64,128]{2,1,0:T(8,128)S(1)} %get-tuple-element.61), channel_id=1, source_target_pairs={{8,0},{16,8},{24,16},{32,24},{40,32},{48,40},{56,48},{64,56},{72,6... | collective-permute-start | bytes 1572872 | tf_op jit(solution)/shard_map/ppermute | solution.py:12
  89.4 16.3 %collective-permute-start.6 = (f32[16,64,128]{2,1,0:T(8,128)S(1)}, f32[16,64,128]{2,1,0:T(8,128)S(1)}, u32[]{:S(2)}, u32[]{:S(2)}) collective-permute-start(f32[16,64,128]{2,1,0:T(8,128)S(1)} %get-tuple-element.64), channel_id=1, source_target_pairs={{0,8},{8,16},{16,24},{24,32},{32,40},{40,48},{48,56},{56,64},{64,7... | collective-permute-start | bytes 1572872 | tf_op jit(solution)/shard_map/ppermute | solution.py:12
  91.4 15.5 %collective-permute-start.7 = (f32[16,64,128]{2,1,0:T(8,128)S(1)}, f32[16,64,128]{2,1,0:T(8,128)S(1)}, u32[]{:S(2)}, u32[]{:S(2)}) collective-permute-start(f32[16,64,128]{2,1,0:T(8,128)S(1)} %get-tuple-element.65), channel_id=1, source_target_pairs={{8,0},{16,8},{24,16},{32,24},{40,32},{48,40},{56,48},{64,56},{72,6... | collective-permute-start | bytes 1572872 | tf_op jit(solution)/shard_map/ppermute | solution.py:12
  107.0 15.3 %collective-permute-start.8 = (f32[16,64,128]{2,1,0:T(8,128)S(1)}, f32[16,64,128]{2,1,0:T(8,128)S(1)}, u32[]{:S(2)}, u32[]{:S(2)}) collective-permute-start(f32[16,64,128]{2,1,0:T(8,128)S(1)} %get-tuple-element.68), channel_id=1, source_target_pairs={{0,8},{8,16},{16,24},{24,32},{32,40},{40,48},{48,56},{56,64},{64,7... | collective-permute-start | bytes 1572872 | tf_op jit(solution)/shard_map/ppermute | solution.py:12
  109.0 14.6 %collective-permute-start.9 = (f32[16,64,128]{2,1,0:T(8,128)S(1)}, f32[16,64,128]{2,1,0:T(8,128)S(1)}, u32[]{:S(2)}, u32[]{:S(2)}) collective-permute-start(f32[16,64,128]{2,1,0:T(8,128)S(1)} %get-tuple-element.69), channel_id=1, source_target_pairs={{8,0},{16,8},{24,16},{32,24},{40,32},{48,40},{56,48},{64,56},{72,6... | collective-permute-start | bytes 1572872 | tf_op jit(solution)/shard_map/ppermute | solution.py:12
  123.7 14.4 %collective-permute-start.10 = (f32[16,64,128]{2,1,0:T(8,128)S(1)}, f32[16,64,128]{2,1,0:T(8,128)S(1)}, u32[]{:S(2)}, u32[]{:S(2)}) collective-permute-start(f32[16,64,128]{2,1,0:T(8,128)S(1)} %get-tuple-element.72), channel_id=1, source_target_pairs={{0,8},{8,16},{16,24},{24,32},{32,40},{40,48},{48,56},{56,64},{64,7... | collective-permute-start | bytes 1572872 | tf_op jit(solution)/shard_map/ppermute | solution.py:12
  125.7 13.7 %collective-permute-start.11 = (f32[16,64,128]{2,1,0:T(8,128)S(1)}, f32[16,64,128]{2,1,0:T(8,128)S(1)}, u32[]{:S(2)}, u32[]{:S(2)}) collective-permute-start(f32[16,64,128]{2,1,0:T(8,128)S(1)} %get-tuple-element.73), channel_id=1, source_target_pairs={{8,0},{16,8},{24,16},{32,24},{40,32},{48,40},{56,48},{64,56},{72,6... | collective-permute-start | bytes 1572872 | tf_op jit(solution)/shard_map/ppermute | solution.py:12
  139.5 13.7 %collective-permute-start.12 = (f32[16,64,128]{2,1,0:T(8,128)S(1)}, f32[16,64,128]{2,1,0:T(8,128)S(1)}, u32[]{:S(2)}, u32[]{:S(2)}) collective-permute-start(f32[16,64,128]{2,1,0:T(8,128)S(1)} %get-tuple-element.76), channel_id=1, source_target_pairs={{0,8},{8,16},{16,24},{24,32},{32,40},{40,48},{48,56},{56,64},{64,7... | collective-permute-start | bytes 1572872 | tf_op jit(solution)/shard_map/ppermute | solution.py:12
  141.4 13.2 %collective-permute-start.13 = (f32[16,64,128]{2,1,0:T(8,128)S(1)}, f32[16,64,128]{2,1,0:T(8,128)S(1)}, u32[]{:S(2)}, u32[]{:S(2)}) collective-permute-start(f32[16,64,128]{2,1,0:T(8,128)S(1)} %get-tuple-element.77), channel_id=1, source_target_pairs={{8,0},{16,8},{24,16},{32,24},{40,32},{48,40},{56,48},{64,56},{72,6... | collective-permute-start | bytes 1572872 | tf_op jit(solution)/shard_map/ppermute | solution.py:12
  154.8 13.7 %collective-permute-start.14 = (f32[16,64,128]{2,1,0:T(8,128)S(1)}, f32[16,64,128]{2,1,0:T(8,128)S(1)}, u32[]{:S(2)}, u32[]{:S(2)}) collective-permute-start(f32[16,64,128]{2,1,0:T(8,128)S(1)} %get-tuple-element.80), channel_id=1, source_target_pairs={{0,8},{8,16},{16,24},{24,32},{32,40},{40,48},{48,56},{56,64},{64,7... | collective-permute-start | bytes 1572872 | tf_op jit(solution)/shard_map/ppermute | solution.py:12
  156.7 13.2 %collective-permute-start.15 = (f32[16,64,128]{2,1,0:T(8,128)S(1)}, f32[16,64,128]{2,1,0:T(8,128)S(1)}, u32[]{:S(2)}, u32[]{:S(2)}) collective-permute-start(f32[16,64,128]{2,1,0:T(8,128)S(1)} %get-tuple-element.81), channel_id=1, source_target_pairs={{8,0},{16,8},{24,16},{32,24},{40,32},{48,40},{56,48},{64,56},{72,6... | collective-permute-start | bytes 1572872 | tf_op jit(solution)/shard_map/ppermute | solution.py:12
  170.1 13.7 %collective-permute-start.16 = (f32[16,64,128]{2,1,0:T(8,128)S(1)}, f32[16,64,128]{2,1,0:T(8,128)S(1)}, u32[]{:S(2)}, u32[]{:S(2)}) collective-permute-start(f32[16,64,128]{2,1,0:T(8,128)S(1)} %get-tuple-element.84), channel_id=1, source_target_pairs={{0,8},{8,16},{16,24},{24,32},{32,40},{40,48},{48,56},{56,64},{64,7... | collective-permute-start | bytes 1572872 | tf_op jit(solution)/shard_map/ppermute | solution.py:12
  172.0 13.2 %collective-permute-start.17 = (f32[16,64,128]{2,1,0:T(8,128)S(1)}, f32[16,64,128]{2,1,0:T(8,128)S(1)}, u32[]{:S(2)}, u32[]{:S(2)}) collective-permute-start(f32[16,64,128]{2,1,0:T(8,128)S(1)} %get-tuple-element.85), channel_id=1, source_target_pairs={{8,0},{16,8},{24,16},{32,24},{40,32},{48,40},{56,48},{64,56},{72,6... | collective-permute-start | bytes 1572872 | tf_op jit(solution)/shard_map/ppermute | solution.py:12
  185.3 14.3 %collective-permute-start.18 = (f32[16,64,128]{2,1,0:T(8,128)S(1)}, f32[16,64,128]{2,1,0:T(8,128)S(1)}, u32[]{:S(2)}, u32[]{:S(2)}) collective-permute-start(f32[16,64,128]{2,1,0:T(8,128)S(1)} %get-tuple-element.88), channel_id=1, source_target_pairs={{0,8},{8,16},{16,24},{24,32},{32,40},{40,48},{48,56},{56,64},{64,7... | collective-permute-start | bytes 1572872 | tf_op jit(solution)/shard_map/ppermute | solution.py:12
  187.3 14.1 %collective-permute-start.19 = (f32[16,64,128]{2,1,0:T(8,128)S(1)}, f32[16,64,128]{2,1,0:T(8,128)S(1)}, u32[]{:S(2)}, u32[]{:S(2)}) collective-permute-start(f32[16,64,128]{2,1,0:T(8,128)S(1)} %get-tuple-element.89), channel_id=1, source_target_pairs={{8,0},{16,8},{24,16},{32,24},{40,32},{48,40},{56,48},{64,56},{72,6... | collective-permute-start | bytes 1572872 | tf_op jit(solution)/shard_map/ppermute | solution.py:12
  201.6 15.4 %collective-permute-start.20 = (f32[16,64,128]{2,1,0:T(8,128)S(1)}, f32[16,64,128]{2,1,0:T(8,128)S(1)}, u32[]{:S(2)}, u32[]{:S(2)}) collective-permute-start(f32[16,64,128]{2,1,0:T(8,128)S(1)} %get-tuple-element.92), channel_id=1, source_target_pairs={{0,8},{8,16},{16,24},{24,32},{32,40},{40,48},{48,56},{56,64},{64,7... | collective-permute-start | bytes 1572872 | tf_op jit(solution)/shard_map/ppermute | solution.py:12
  203.5 15.2 %collective-permute-start.21 = (f32[16,64,128]{2,1,0:T(8,128)S(1)}, f32[16,64,128]{2,1,0:T(8,128)S(1)}, u32[]{:S(2)}, u32[]{:S(2)}) collective-permute-start(f32[16,64,128]{2,1,0:T(8,128)S(1)} %get-tuple-element.93), channel_id=1, source_target_pairs={{8,0},{16,8},{24,16},{32,24},{40,32},{48,40},{56,48},{64,56},{72,6... | collective-permute-start | bytes 1572872 | tf_op jit(solution)/shard_map/ppermute | solution.py:12
  210.1 0.6 copy-start.14
  210.2 2.0 copy-start.8
  212.2 15.4 %copy-start.10 = (f32[16,128]{1,0:T(8,128)}, f32[16,128]{1,0:T(8,128)S(1)}, u32[]{:S(2)}) copy-start(f32[16,128]{1,0:T(8,128)S(1)} %get-tuple-element.116) | copy-start | bytes 24580
  218.8 13.7 %collective-permute-start.22 = (f32[16,64,128]{2,1,0:T(8,128)S(1)}, f32[16,64,128]{2,1,0:T(8,128)S(1)}, u32[]{:S(2)}, u32[]{:S(2)}) collective-permute-start(f32[16,64,128]{2,1,0:T(8,128)S(1)} %get-tuple-element.96), channel_id=1, source_target_pairs={{0,8},{8,16},{16,24},{24,32},{32,40},{40,48},{48,56},{56,64},{64,7... | collective-permute-start | bytes 1572872 | tf_op jit(solution)/shard_map/ppermute | solution.py:12
  221.0 13.0 %collective-permute-start.23 = (f32[16,64,128]{2,1,0:T(8,128)S(1)}, f32[16,64,128]{2,1,0:T(8,128)S(1)}, u32[]{:S(2)}, u32[]{:S(2)}) collective-permute-start(f32[16,64,128]{2,1,0:T(8,128)S(1)} %get-tuple-element.97), channel_id=1, source_target_pairs={{8,0},{16,8},{24,16},{32,24},{40,32},{48,40},{56,48},{64,56},{72,6... | collective-permute-start | bytes 1572872 | tf_op jit(solution)/shard_map/ppermute | solution.py:12
  229.4 0.7 copy-start.6
  229.4 0.9 copy-start.9
  229.4 0.9 copy-start.15
  231.6 2.8 copy-start.3
  237.1 0.7 copy-start.22
  238.1 0.7 copy-start.7
  238.1 0.7 copy-start.16
  242.1 1.0 copy-start.4
  242.1 1.0 copy-start.11
  242.2 1.0 copy-start.12
  242.2 1.0 copy-start.13
  243.2 0.7 copy-start.21
Sparse Core Ops, SparseCore 0:
  237.2 32.9 reduce-scatter.1
where the time goes:
time: 280 us; the launch traced here: 278 us
  waiting for transfers between devices  119 us (42%)
  starting transfers between devices  106 us (38%)
  between operations  14.6 us (5%)
  blocking collectives  13.3 us (5%)
  matrix products  10.1 us (4%)
  local copies, waits for them, and re-layouts  8.7 us (3%)
  other arithmetic  6.84 us (2%)
    ppermute x24, starting transfers between devices, from_behind(): return lax.ppermute(x, axis, pairs)  106 us
    ppermute x24, waiting for transfers between devices, from_behind(): return lax.ppermute(x, axis, pairs)  93.1 us
    reduce_scatter x1, waiting for transfers between devices, local(): lax.psum_scatter(jnp.stack([gb, gc]), 'tensor', scatter_dimension=1, tile...  25.7 us
    all_gather x1, blocking collectives, local(): lax.all_gather(jnp.stack([b_rows, c_rows]), 'tensor', axis=1, tiled=True)  13.3 us
  transfers between devices with their start and end apart: 25, of which 25 were waited for; matrix products, arithmetic and copies ran while one was open for 4% of the time, Pallas kernels for 0%

commit v1 on v0

--- a/solution.py
+++ b/solution.py
@@ -16,7 +16,9 @@
     length = inputs.shape[0]
     heads = step_size.shape[0]
     width = inputs.shape[1] // heads
-    rows = lax.all_gather(jnp.stack([b_rows, c_rows]), "tensor", axis=1, tiled=True)
+    value = jnp.stack([b_rows, c_rows])
+    sent = jnp.stack([value] * lax.axis_size("tensor"))
+    rows = jnp.concatenate(lax.all_to_all(sent, "tensor", 0, 0), axis=1)
     b_bf, c_bf = (rows[0], rows[1])
     bmat = b_bf.astype(jnp.float32)
     cmat = c_bf.astype(jnp.float32)

time: 280 us -> 272 us (0.971)
  blocking collectives: 13.3 us -> 0 us
  starting transfers between devices: 106 us -> 111 us
  waiting for transfers between devices: 119 us -> 122 us
    all_gather x1 -> x0, blocking collectives: 13.3 us -> none  [local(): lax.all_gather(jnp.stack([b_rows, c_rows]), 'tensor', axis=1, tiled=True)]
    all_to_all x0 -> x1, starting transfers between devices: none -> 4.47 us  [local(): rows = jnp.concatenate(lax.all_to_all(sent, 'tensor', 0, 0), axis=1)]
  transfers between devices with their start and end apart: 25 -> 26, of which waited for: 25 -> 26; matrix products, arithmetic and copies ran while one was open for 4% -> 5% of each run, Pallas kernels for 0% -> 0%
where the time goes in v1:
time: 272 us; the launch traced here: 271 us
  waiting for transfers between devices  122 us (45%)
  starting transfers between devices  111 us (41%)
  between operations  14.5 us (5%)
  matrix products  10.1 us (4%)
  other arithmetic  7.2 us (3%)
  local copies, waits for them, and re-layouts  6.95 us (3%)
    ppermute x24, starting transfers between devices, from_behind(): return lax.ppermute(x, axis, pairs)  106 us
    ppermute x24, waiting for transfers between devices, from_behind(): return lax.ppermute(x, axis, pairs)  93.2 us
    reduce_scatter x1, waiting for transfers between devices, local(): lax.psum_scatter(jnp.stack([gb, gc]), 'tensor', scatter_dimension=1, tile...  27.7 us
  transfers between devices with their start and end apart: 26, of which 26 were waited for; matrix products, arithmetic and copies ran while one was open for 5% of the time, Pallas kernels for 0%

profile of v1, /device:TPU:2, one launch (start us, length us, event | category | flops | bytes accessed | tf_op | source)
XLA Modules:
  0.0 271.0 jit_solution(12189318835786711779)
XLA Ops:
  8.6 4.5 %all-to-all-start = ((bf16[8,2,16,128]{3,2,1,0:T(8,128)(2,1)}), bf16[8,2,16,128]{3,2,1,0:T(8,128)(2,1)S(1)}, u32[]{:S(2)}, u32[]{:S(2)}) async-start(bf16[8,2,16,128]{3,2,1,0:T(8,128)(2,1)} %stack.32), calls=%async_computation | async-start | bytes 131072 | tf_op jit(solution)/shard_map/all_to_all | solution.py:21
  19.5 3.8 %collective-permute-start = (f32[16,64,128]{2,1,0:T(8,128)S(1)}, f32[16,64,128]{2,1,0:T(8,128)S(1)}, u32[]{:S(2)}, u32[]{:S(2)}) collective-permute-start(f32[16,64,128]{2,1,0:T(8,128)S(1)} %get-tuple-element.52), channel_id=1, source_target_pairs={{0,8},{8,16},{16,24},{24,32},{32,40},{40,48},{48,56},{56,64},{64,7... | collective-permute-start | bytes 1572872 | tf_op jit(solution)/shard_map/ppermute | solution.py:12
  23.3 9.5 %collective-permute-start.1 = (f32[16,64,128]{2,1,0:T(8,128)S(1)}, f32[16,64,128]{2,1,0:T(8,128)S(1)}, u32[]{:S(2)}, u32[]{:S(2)}) collective-permute-start(f32[16,64,128]{2,1,0:T(8,128)S(1)} %get-tuple-element.53), channel_id=1, source_target_pairs={{8,0},{16,8},{24,16},{32,24},{40,32},{48,40},{56,48},{64,56},{72,6... | collective-permute-start | bytes 1572872 | tf_op jit(solution)/shard_map/ppermute | solution.py:12
  32.8 9.9 %collective-permute-done = f32[16,64,128]{2,1,0:T(8,128)S(1)} collective-permute-done((f32[16,64,128]{2,1,0:T(8,128)S(1)}, f32[16,64,128]{2,1,0:T(8,128)S(1)}, u32[]{:S(2)}, u32[]{:S(2)}) %collective-permute-start) | collective-permute-done | bytes 524320 | tf_op jit(solution)/shard_map/ppermute | solution.py:12
  44.0 1.9 collective-permute-start.2
  45.9 6.5 %collective-permute-start.3 = (f32[16,64,128]{2,1,0:T(8,128)S(1)}, f32[16,64,128]{2,1,0:T(8,128)S(1)}, u32[]{:S(2)}, u32[]{:S(2)}) collective-permute-start(f32[16,64,128]{2,1,0:T(8,128)S(1)} %get-tuple-element.57), channel_id=1, source_target_pairs={{8,0},{16,8},{24,16},{32,24},{40,32},{48,40},{56,48},{64,56},{72,6... | collective-permute-start | bytes 1572872 | tf_op jit(solution)/shard_map/ppermute | solution.py:12
  52.4 9.0 %collective-permute-done.2 = f32[16,64,128]{2,1,0:T(8,128)S(1)} collective-permute-done((f32[16,64,128]{2,1,0:T(8,128)S(1)}, f32[16,64,128]{2,1,0:T(8,128)S(1)}, u32[]{:S(2)}, u32[]{:S(2)}) %collective-permute-start.2) | collective-permute-done | bytes 524320 | tf_op jit(solution)/shard_map/ppermute | solution.py:12
  62.8 1.9 collective-permute-start.4
  64.7 6.5 %collective-permute-start.5 = (f32[16,64,128]{2,1,0:T(8,128)S(1)}, f32[16,64,128]{2,1,0:T(8,128)S(1)}, u32[]{:S(2)}, u32[]{:S(2)}) collective-permute-start(f32[16,64,128]{2,1,0:T(8,128)S(1)} %get-tuple-element.61), channel_id=1, source_target_pairs={{8,0},{16,8},{24,16},{32,24},{40,32},{48,40},{56,48},{64,56},{72,6... | collective-permute-start | bytes 1572872 | tf_op jit(solution)/shard_map/ppermute | solution.py:12
  71.2 8.1 %collective-permute-done.4 = f32[16,64,128]{2,1,0:T(8,128)S(1)} collective-permute-done((f32[16,64,128]{2,1,0:T(8,128)S(1)}, f32[16,64,128]{2,1,0:T(8,128)S(1)}, u32[]{:S(2)}, u32[]{:S(2)}) %collective-permute-start.4) | collective-permute-done | bytes 524320 | tf_op jit(solution)/shard_map/ppermute | solution.py:12
  80.7 1.9 collective-permute-start.6
  82.6 6.5 %collective-permute-start.7 = (f32[16,64,128]{2,1,0:T(8,128)S(1)}, f32[16,64,128]{2,1,0:T(8,128)S(1)}, u32[]{:S(2)}, u32[]{:S(2)}) collective-permute-start(f32[16,64,128]{2,1,0:T(8,128)S(1)} %get-tuple-element.65), channel_id=1, source_target_pairs={{8,0},{16,8},{24,16},{32,24},{40,32},{48,40},{56,48},{64,56},{72,6... | collective-permute-start | bytes 1572872 | tf_op jit(solution)/shard_map/ppermute | solution.py:12
  89.1 7.2 %collective-permute-done.6 = f32[16,64,128]{2,1,0:T(8,128)S(1)} collective-permute-done((f32[16,64,128]{2,1,0:T(8,128)S(1)}, f32[16,64,128]{2,1,0:T(8,128)S(1)}, u32[]{:S(2)}, u32[]{:S(2)}) %collective-permute-start.6) | collective-permute-done | bytes 524320 | tf_op jit(solution)/shard_map/ppermute | solution.py:12
  97.6 1.9 collective-permute-start.8
  99.5 6.5 %collective-permute-start.9 = (f32[16,64,128]{2,1,0:T(8,128)S(1)}, f32[16,64,128]{2,1,0:T(8,128)S(1)}, u32[]{:S(2)}, u32[]{:S(2)}) collective-permute-start(f32[16,64,128]{2,1,0:T(8,128)S(1)} %get-tuple-element.69), channel_id=1, source_target_pairs={{8,0},{16,8},{24,16},{32,24},{40,32},{48,40},{56,48},{64,56},{72,6... | collective-permute-start | bytes 1572872 | tf_op jit(solution)/shard_map/ppermute | solution.py:12
  106.0 6.2 %collective-permute-done.8 = f32[16,64,128]{2,1,0:T(8,128)S(1)} collective-permute-done((f32[16,64,128]{2,1,0:T(8,128)S(1)}, f32[16,64,128]{2,1,0:T(8,128)S(1)}, u32[]{:S(2)}, u32[]{:S(2)}) %collective-permute-start.8) | collective-permute-done | bytes 524320 | tf_op jit(solution)/shard_map/ppermute | solution.py:12
  113.6 1.9 collective-permute-start.10
  115.6 6.5 %collective-permute-start.11 = (f32[16,64,128]{2,1,0:T(8,128)S(1)}, f32[16,64,128]{2,1,0:T(8,128)S(1)}, u32[]{:S(2)}, u32[]{:S(2)}) collective-permute-start(f32[16,64,128]{2,1,0:T(8,128)S(1)} %get-tuple-element.73), channel_id=1, source_target_pairs={{8,0},{16,8},{24,16},{32,24},{40,32},{48,40},{56,48},{64,56},{72,6... | collective-permute-start | bytes 1572872 | tf_op jit(solution)/shard_map/ppermute | solution.py:12
  122.1 5.3 %collective-permute-done.10 = f32[16,64,128]{2,1,0:T(8,128)S(1)} collective-permute-done((f32[16,64,128]{2,1,0:T(8,128)S(1)}, f32[16,64,128]{2,1,0:T(8,128)S(1)}, u32[]{:S(2)}, u32[]{:S(2)}) %collective-permute-start.10) | collective-permute-done | bytes 524320 | tf_op jit(solution)/shard_map/ppermute | solution.py:12
  127.4 1.4 collective-permute-done.11
  128.9 1.9 collective-permute-start.12
  130.8 6.5 %collective-permute-start.13 = (f32[16,64,128]{2,1,0:T(8,128)S(1)}, f32[16,64,128]{2,1,0:T(8,128)S(1)}, u32[]{:S(2)}, u32[]{:S(2)}) collective-permute-start(f32[16,64,128]{2,1,0:T(8,128)S(1)} %get-tuple-element.77), channel_id=1, source_target_pairs={{8,0},{16,8},{24,16},{32,24},{40,32},{48,40},{56,48},{64,56},{72,6... | collective-permute-start | bytes 1572872 | tf_op jit(solution)/shard_map/ppermute | solution.py:12
  137.3 5.2 %collective-permute-done.12 = f32[16,64,128]{2,1,0:T(8,128)S(1)} collective-permute-done((f32[16,64,128]{2,1,0:T(8,128)S(1)}, f32[16,64,128]{2,1,0:T(8,128)S(1)}, u32[]{:S(2)}, u32[]{:S(2)}) %collective-permute-start.12) | collective-permute-done | bytes 524320 | tf_op jit(solution)/shard_map/ppermute | solution.py:12
  142.6 1.5 collective-permute-done.13
  144.2 1.9 collective-permute-start.14
  146.1 6.5 %collective-permute-start.15 = (f32[16,64,128]{2,1,0:T(8,128)S(1)}, f32[16,64,128]{2,1,0:T(8,128)S(1)}, u32[]{:S(2)}, u32[]{:S(2)}) collective-permute-start(f32[16,64,128]{2,1,0:T(8,128)S(1)} %get-tuple-element.81), channel_id=1, source_target_pairs={{8,0},{16,8},{24,16},{32,24},{40,32},{48,40},{56,48},{64,56},{72,6... | collective-permute-start | bytes 1572872 | tf_op jit(solution)/shard_map/ppermute | solution.py:12
  152.6 5.2 %collective-permute-done.14 = f32[16,64,128]{2,1,0:T(8,128)S(1)} collective-permute-done((f32[16,64,128]{2,1,0:T(8,128)S(1)}, f32[16,64,128]{2,1,0:T(8,128)S(1)}, u32[]{:S(2)}, u32[]{:S(2)}) %collective-permute-start.14) | collective-permute-done | bytes 524320 | tf_op jit(solution)/shard_map/ppermute | solution.py:12
  157.8 1.5 collective-permute-done.15
  159.5 1.9 collective-permute-start.16
  161.4 6.5 %collective-permute-start.17 = (f32[16,64,128]{2,1,0:T(8,128)S(1)}, f32[16,64,128]{2,1,0:T(8,128)S(1)}, u32[]{:S(2)}, u32[]{:S(2)}) collective-permute-start(f32[16,64,128]{2,1,0:T(8,128)S(1)} %get-tuple-element.85), channel_id=1, source_target_pairs={{8,0},{16,8},{24,16},{32,24},{40,32},{48,40},{56,48},{64,56},{72,6... | collective-permute-start | bytes 1572872 | tf_op jit(solution)/shard_map/ppermute | solution.py:12
  167.9 5.6 %collective-permute-done.16 = f32[16,64,128]{2,1,0:T(8,128)S(1)} collective-permute-done((f32[16,64,128]{2,1,0:T(8,128)S(1)}, f32[16,64,128]{2,1,0:T(8,128)S(1)}, u32[]{:S(2)}, u32[]{:S(2)}) %collective-permute-start.16) | collective-permute-done | bytes 524320 | tf_op jit(solution)/shard_map/ppermute | solution.py:12
  173.5 1.7 collective-permute-done.17
  175.4 1.9 collective-permute-start.18
  177.4 6.5 %collective-permute-start.19 = (f32[16,64,128]{2,1,0:T(8,128)S(1)}, f32[16,64,128]{2,1,0:T(8,128)S(1)}, u32[]{:S(2)}, u32[]{:S(2)}) collective-permute-start(f32[16,64,128]{2,1,0:T(8,128)S(1)} %get-tuple-element.89), channel_id=1, source_target_pairs={{8,0},{16,8},{24,16},{32,24},{40,32},{48,40},{56,48},{64,56},{72,6... | collective-permute-start | bytes 1572872 | tf_op jit(solution)/shard_map/ppermute | solution.py:12
  183.9 6.7 %collective-permute-done.18 = f32[16,64,128]{2,1,0:T(8,128)S(1)} collective-permute-done((f32[16,64,128]{2,1,0:T(8,128)S(1)}, f32[16,64,128]{2,1,0:T(8,128)S(1)}, u32[]{:S(2)}, u32[]{:S(2)}) %collective-permute-start.18) | collective-permute-done | bytes 524320 | tf_op jit(solution)/shard_map/ppermute | solution.py:12
  190.5 1.7 collective-permute-done.19
  192.5 2.5 collective-permute-start.20
  194.9 6.0 %collective-permute-start.21 = (f32[16,64,128]{2,1,0:T(8,128)S(1)}, f32[16,64,128]{2,1,0:T(8,128)S(1)}, u32[]{:S(2)}, u32[]{:S(2)}) collective-permute-start(f32[16,64,128]{2,1,0:T(8,128)S(1)} %get-tuple-element.93), channel_id=1, source_target_pairs={{8,0},{16,8},{24,16},{32,24},{40,32},{48,40},{56,48},{64,56},{72,6... | collective-permute-start | bytes 1572872 | tf_op jit(solution)/shard_map/ppermute | solution.py:12
  201.1 1.6 fusion.12
  202.7 5.0 %collective-permute-done.20 = f32[16,64,128]{2,1,0:T(8,128)S(1)} collective-permute-done((f32[16,64,128]{2,1,0:T(8,128)S(1)}, f32[16,64,128]{2,1,0:T(8,128)S(1)}, u32[]{:S(2)}, u32[]{:S(2)}) %collective-permute-start.20) | collective-permute-done | bytes 524320 | tf_op jit(solution)/shard_map/ppermute | solution.py:12
  207.7 1.9 collective-permute-done.21
  210.6 4.1 %collective-permute-start.22 = (f32[16,64,128]{2,1,0:T(8,128)}, f32[16,64,128]{2,1,0:T(8,128)S(1)}, u32[]{:S(2)}, u32[]{:S(2)}) collective-permute-start(f32[16,64,128]{2,1,0:T(8,128)} %get-tuple-element.96), channel_id=1, source_target_pairs={{0,8},{8,16},{16,24},{24,32},{32,40},{40,48},{48,56},{56,64},{64,7... | collective-permute-start | bytes 1572872 | tf_op jit(solution)/shard_map/ppermute | solution.py:12
  214.7 4.5 %collective-permute-start.23 = (f32[16,64,128]{2,1,0:T(8,128)S(1)}, f32[16,64,128]{2,1,0:T(8,128)S(1)}, u32[]{:S(2)}, u32[]{:S(2)}) collective-permute-start(f32[16,64,128]{2,1,0:T(8,128)S(1)} %get-tuple-element.97), channel_id=1, source_target_pairs={{8,0},{16,8},{24,16},{32,24},{40,32},{48,40},{56,48},{64,56},{72,6... | collective-permute-start | bytes 1572872 | tf_op jit(solution)/shard_map/ppermute | solution.py:12
  220.2 1.3 fusion.10
  221.5 2.9 %collective-permute-done.22 = f32[16,64,128]{2,1,0:T(8,128)S(1)} collective-permute-done((f32[16,64,128]{2,1,0:T(8,128)}, f32[16,64,128]{2,1,0:T(8,128)S(1)}, u32[]{:S(2)}, u32[]{:S(2)}) %collective-permute-start.22) | collective-permute-done | bytes 524320 | tf_op jit(solution)/shard_map/ppermute | solution.py:12
  224.4 1.3 collective-permute-done.23
  231.4 1.9 fusion.7
  235.2 27.7 %reduce-scatter.2.cloned.1.call-done = f32[2,16,128]{2,1,0:T(8,128)} async-done(((f32[2,128,128]{2,1,0:T(8,128)}), f32[2,16,128]{2,1,0:T(8,128)}) %reduce-scatter.2.cloned.1.call-update) | async-done | bytes 16400 | tf_op jit(solution)/shard_map/reduce_scatter | solution.py:86
  (69 shorter events, 26.2 us)
Async XLA Ops:
  7.2 9.6 %copy-start.1 = (bf16[128,1024]{1,0:T(8,128)(2,1)S(1)}, bf16[128,1024]{1,0:T(8,128)(2,1)}, u32[]{:S(2)}) copy-start(bf16[128,1024]{1,0:T(8,128)(2,1)} %param.8) | copy-start | bytes 786436
  8.6 10.1 %all-to-all-start = ((bf16[8,2,16,128]{3,2,1,0:T(8,128)(2,1)}), bf16[8,2,16,128]{3,2,1,0:T(8,128)(2,1)S(1)}, u32[]{:S(2)}, u32[]{:S(2)}) async-start(bf16[8,2,16,128]{3,2,1,0:T(8,128)(2,1)} %stack.32), calls=%async_computation | async-start | bytes 131072 | tf_op jit(solution)/shard_map/all_to_all | solution.py:21
  13.0 249.8 %reduce-scatter.2.cloned.1.call-start = ((), (), s32[]{:S(2)}) async-start(), calls=%async_computation.2 | async-start | bytes 147456 | tf_op jit(solution)/shard_map/reduce_scatter | solution.py:86
  13.9 0.7 copy-start.3
  14.0 1.9 copy-start
  15.3 0.7 copy-start.4
  16.8 1.0 copy-start.2
  19.5 23.2 %collective-permute-start = (f32[16,64,128]{2,1,0:T(8,128)S(1)}, f32[16,64,128]{2,1,0:T(8,128)S(1)}, u32[]{:S(2)}, u32[]{:S(2)}) collective-permute-start(f32[16,64,128]{2,1,0:T(8,128)S(1)} %get-tuple-element.52), channel_id=1, source_target_pairs={{0,8},{8,16},{16,24},{24,32},{32,40},{40,48},{48,56},{56,64},{64,7... | collective-permute-start | bytes 1572872 | tf_op jit(solution)/shard_map/ppermute | solution.py:12
  23.3 20.5 %collective-permute-start.1 = (f32[16,64,128]{2,1,0:T(8,128)S(1)}, f32[16,64,128]{2,1,0:T(8,128)S(1)}, u32[]{:S(2)}, u32[]{:S(2)}) collective-permute-start(f32[16,64,128]{2,1,0:T(8,128)S(1)} %get-tuple-element.53), channel_id=1, source_target_pairs={{8,0},{16,8},{24,16},{32,24},{40,32},{48,40},{56,48},{64,56},{72,6... | collective-permute-start | bytes 1572872 | tf_op jit(solution)/shard_map/ppermute | solution.py:12
  44.0 17.4 %collective-permute-start.2 = (f32[16,64,128]{2,1,0:T(8,128)S(1)}, f32[16,64,128]{2,1,0:T(8,128)S(1)}, u32[]{:S(2)}, u32[]{:S(2)}) collective-permute-start(f32[16,64,128]{2,1,0:T(8,128)S(1)} %get-tuple-element.56), channel_id=1, source_target_pairs={{0,8},{8,16},{16,24},{24,32},{32,40},{40,48},{48,56},{56,64},{64,7... | collective-permute-start | bytes 1572872 | tf_op jit(solution)/shard_map/ppermute | solution.py:12
  45.9 16.7 %collective-permute-start.3 = (f32[16,64,128]{2,1,0:T(8,128)S(1)}, f32[16,64,128]{2,1,0:T(8,128)S(1)}, u32[]{:S(2)}, u32[]{:S(2)}) collective-permute-start(f32[16,64,128]{2,1,0:T(8,128)S(1)} %get-tuple-element.57), channel_id=1, source_target_pairs={{8,0},{16,8},{24,16},{32,24},{40,32},{48,40},{56,48},{64,56},{72,6... | collective-permute-start | bytes 1572872 | tf_op jit(solution)/shard_map/ppermute | solution.py:12
  62.8 16.5 %collective-permute-start.4 = (f32[16,64,128]{2,1,0:T(8,128)S(1)}, f32[16,64,128]{2,1,0:T(8,128)S(1)}, u32[]{:S(2)}, u32[]{:S(2)}) collective-permute-start(f32[16,64,128]{2,1,0:T(8,128)S(1)} %get-tuple-element.60), channel_id=1, source_target_pairs={{0,8},{8,16},{16,24},{24,32},{32,40},{40,48},{48,56},{56,64},{64,7... | collective-permute-start | bytes 1572872 | tf_op jit(solution)/shard_map/ppermute | solution.py:12
  64.7 15.8 %collective-permute-start.5 = (f32[16,64,128]{2,1,0:T(8,128)S(1)}, f32[16,64,128]{2,1,0:T(8,128)S(1)}, u32[]{:S(2)}, u32[]{:S(2)}) collective-permute-start(f32[16,64,128]{2,1,0:T(8,128)S(1)} %get-tuple-element.61), channel_id=1, source_target_pairs={{8,0},{16,8},{24,16},{32,24},{40,32},{48,40},{56,48},{64,56},{72,6... | collective-permute-start | bytes 1572872 | tf_op jit(solution)/shard_map/ppermute | solution.py:12
  80.7 15.6 %collective-permute-start.6 = (f32[16,64,128]{2,1,0:T(8,128)S(1)}, f32[16,64,128]{2,1,0:T(8,128)S(1)}, u32[]{:S(2)}, u32[]{:S(2)}) collective-permute-start(f32[16,64,128]{2,1,0:T(8,128)S(1)} %get-tuple-element.64), channel_id=1, source_target_pairs={{0,8},{8,16},{16,24},{24,32},{32,40},{40,48},{48,56},{56,64},{64,7... | collective-permute-start | bytes 1572872 | tf_op jit(solution)/shard_map/ppermute | solution.py:12
  82.6 14.8 %collective-permute-start.7 = (f32[16,64,128]{2,1,0:T(8,128)S(1)}, f32[16,64,128]{2,1,0:T(8,128)S(1)}, u32[]{:S(2)}, u32[]{:S(2)}) collective-permute-start(f32[16,64,128]{2,1,0:T(8,128)S(1)} %get-tuple-element.65), channel_id=1, source_target_pairs={{8,0},{16,8},{24,16},{32,24},{40,32},{48,40},{56,48},{64,56},{72,6... | collective-permute-start | bytes 1572872 | tf_op jit(solution)/shard_map/ppermute | solution.py:12
  97.6 14.7 %collective-permute-start.8 = (f32[16,64,128]{2,1,0:T(8,128)S(1)}, f32[16,64,128]{2,1,0:T(8,128)S(1)}, u32[]{:S(2)}, u32[]{:S(2)}) collective-permute-start(f32[16,64,128]{2,1,0:T(8,128)S(1)} %get-tuple-element.68), channel_id=1, source_target_pairs={{0,8},{8,16},{16,24},{24,32},{32,40},{40,48},{48,56},{56,64},{64,7... | collective-permute-start | bytes 1572872 | tf_op jit(solution)/shard_map/ppermute | solution.py:12
  99.5 13.9 %collective-permute-start.9 = (f32[16,64,128]{2,1,0:T(8,128)S(1)}, f32[16,64,128]{2,1,0:T(8,128)S(1)}, u32[]{:S(2)}, u32[]{:S(2)}) collective-permute-start(f32[16,64,128]{2,1,0:T(8,128)S(1)} %get-tuple-element.69), channel_id=1, source_target_pairs={{8,0},{16,8},{24,16},{32,24},{40,32},{48,40},{56,48},{64,56},{72,6... | collective-permute-start | bytes 1572872 | tf_op jit(solution)/shard_map/ppermute | solution.py:12
  113.6 13.7 %collective-permute-start.10 = (f32[16,64,128]{2,1,0:T(8,128)S(1)}, f32[16,64,128]{2,1,0:T(8,128)S(1)}, u32[]{:S(2)}, u32[]{:S(2)}) collective-permute-start(f32[16,64,128]{2,1,0:T(8,128)S(1)} %get-tuple-element.72), channel_id=1, source_target_pairs={{0,8},{8,16},{16,24},{24,32},{32,40},{40,48},{48,56},{56,64},{64,7... | collective-permute-start | bytes 1572872 | tf_op jit(solution)/shard_map/ppermute | solution.py:12
  115.6 13.2 %collective-permute-start.11 = (f32[16,64,128]{2,1,0:T(8,128)S(1)}, f32[16,64,128]{2,1,0:T(8,128)S(1)}, u32[]{:S(2)}, u32[]{:S(2)}) collective-permute-start(f32[16,64,128]{2,1,0:T(8,128)S(1)} %get-tuple-element.73), channel_id=1, source_target_pairs={{8,0},{16,8},{24,16},{32,24},{40,32},{48,40},{56,48},{64,56},{72,6... | collective-permute-start | bytes 1572872 | tf_op jit(solution)/shard_map/ppermute | solution.py:12
  128.9 13.7 %collective-permute-start.12 = (f32[16,64,128]{2,1,0:T(8,128)S(1)}, f32[16,64,128]{2,1,0:T(8,128)S(1)}, u32[]{:S(2)}, u32[]{:S(2)}) collective-permute-start(f32[16,64,128]{2,1,0:T(8,128)S(1)} %get-tuple-element.76), channel_id=1, source_target_pairs={{0,8},{8,16},{16,24},{24,32},{32,40},{40,48},{48,56},{56,64},{64,7... | collective-permute-start | bytes 1572872 | tf_op jit(solution)/shard_map/ppermute | solution.py:12
  130.8 13.2 %collective-permute-start.13 = (f32[16,64,128]{2,1,0:T(8,128)S(1)}, f32[16,64,128]{2,1,0:T(8,128)S(1)}, u32[]{:S(2)}, u32[]{:S(2)}) collective-permute-start(f32[16,64,128]{2,1,0:T(8,128)S(1)} %get-tuple-element.77), channel_id=1, source_target_pairs={{8,0},{16,8},{24,16},{32,24},{40,32},{48,40},{56,48},{64,56},{72,6... | collective-permute-start | bytes 1572872 | tf_op jit(solution)/shard_map/ppermute | solution.py:12
  144.2 13.7 %collective-permute-start.14 = (f32[16,64,128]{2,1,0:T(8,128)S(1)}, f32[16,64,128]{2,1,0:T(8,128)S(1)}, u32[]{:S(2)}, u32[]{:S(2)}) collective-permute-start(f32[16,64,128]{2,1,0:T(8,128)S(1)} %get-tuple-element.80), channel_id=1, source_target_pairs={{0,8},{8,16},{16,24},{24,32},{32,40},{40,48},{48,56},{56,64},{64,7... | collective-permute-start | bytes 1572872 | tf_op jit(solution)/shard_map/ppermute | solution.py:12
  146.1 13.2 %collective-permute-start.15 = (f32[16,64,128]{2,1,0:T(8,128)S(1)}, f32[16,64,128]{2,1,0:T(8,128)S(1)}, u32[]{:S(2)}, u32[]{:S(2)}) collective-permute-start(f32[16,64,128]{2,1,0:T(8,128)S(1)} %get-tuple-element.81), channel_id=1, source_target_pairs={{8,0},{16,8},{24,16},{32,24},{40,32},{48,40},{56,48},{64,56},{72,6... | collective-permute-start | bytes 1572872 | tf_op jit(solution)/shard_map/ppermute | solution.py:12
  159.5 14.0 %collective-permute-start.16 = (f32[16,64,128]{2,1,0:T(8,128)S(1)}, f32[16,64,128]{2,1,0:T(8,128)S(1)}, u32[]{:S(2)}, u32[]{:S(2)}) collective-permute-start(f32[16,64,128]{2,1,0:T(8,128)S(1)} %get-tuple-element.84), channel_id=1, source_target_pairs={{0,8},{8,16},{16,24},{24,32},{32,40},{40,48},{48,56},{56,64},{64,7... | collective-permute-start | bytes 1572872 | tf_op jit(solution)/shard_map/ppermute | solution.py:12
  161.4 13.8 %collective-permute-start.17 = (f32[16,64,128]{2,1,0:T(8,128)S(1)}, f32[16,64,128]{2,1,0:T(8,128)S(1)}, u32[]{:S(2)}, u32[]{:S(2)}) collective-permute-start(f32[16,64,128]{2,1,0:T(8,128)S(1)} %get-tuple-element.85), channel_id=1, source_target_pairs={{8,0},{16,8},{24,16},{32,24},{40,32},{48,40},{56,48},{64,56},{72,6... | collective-permute-start | bytes 1572872 | tf_op jit(solution)/shard_map/ppermute | solution.py:12
  175.4 15.1 %collective-permute-start.18 = (f32[16,64,128]{2,1,0:T(8,128)S(1)}, f32[16,64,128]{2,1,0:T(8,128)S(1)}, u32[]{:S(2)}, u32[]{:S(2)}) collective-permute-start(f32[16,64,128]{2,1,0:T(8,128)S(1)} %get-tuple-element.88), channel_id=1, source_target_pairs={{0,8},{8,16},{16,24},{24,32},{32,40},{40,48},{48,56},{56,64},{64,7... | collective-permute-start | bytes 1572872 | tf_op jit(solution)/shard_map/ppermute | solution.py:12
  177.4 14.9 %collective-permute-start.19 = (f32[16,64,128]{2,1,0:T(8,128)S(1)}, f32[16,64,128]{2,1,0:T(8,128)S(1)}, u32[]{:S(2)}, u32[]{:S(2)}) collective-permute-start(f32[16,64,128]{2,1,0:T(8,128)S(1)} %get-tuple-element.89), channel_id=1, source_target_pairs={{8,0},{16,8},{24,16},{32,24},{40,32},{48,40},{56,48},{64,56},{72,6... | collective-permute-start | bytes 1572872 | tf_op jit(solution)/shard_map/ppermute | solution.py:12
  192.5 15.2 %collective-permute-start.20 = (f32[16,64,128]{2,1,0:T(8,128)S(1)}, f32[16,64,128]{2,1,0:T(8,128)S(1)}, u32[]{:S(2)}, u32[]{:S(2)}) collective-permute-start(f32[16,64,128]{2,1,0:T(8,128)S(1)} %get-tuple-element.92), channel_id=1, source_target_pairs={{0,8},{8,16},{16,24},{24,32},{32,40},{40,48},{48,56},{56,64},{64,7... | collective-permute-start | bytes 1572872 | tf_op jit(solution)/shard_map/ppermute | solution.py:12
  194.9 14.7 %collective-permute-start.21 = (f32[16,64,128]{2,1,0:T(8,128)S(1)}, f32[16,64,128]{2,1,0:T(8,128)S(1)}, u32[]{:S(2)}, u32[]{:S(2)}) collective-permute-start(f32[16,64,128]{2,1,0:T(8,128)S(1)} %get-tuple-element.93), channel_id=1, source_target_pairs={{8,0},{16,8},{24,16},{32,24},{40,32},{48,40},{56,48},{64,56},{72,6... | collective-permute-start | bytes 1572872 | tf_op jit(solution)/shard_map/ppermute | solution.py:12
  210.6 13.8 %collective-permute-start.22 = (f32[16,64,128]{2,1,0:T(8,128)}, f32[16,64,128]{2,1,0:T(8,128)S(1)}, u32[]{:S(2)}, u32[]{:S(2)}) collective-permute-start(f32[16,64,128]{2,1,0:T(8,128)} %get-tuple-element.96), channel_id=1, source_target_pairs={{0,8},{8,16},{16,24},{24,32},{32,40},{40,48},{48,56},{56,64},{64,7... | collective-permute-start | bytes 1572872 | tf_op jit(solution)/shard_map/ppermute | solution.py:12
  214.7 11.1 %collective-permute-start.23 = (f32[16,64,128]{2,1,0:T(8,128)S(1)}, f32[16,64,128]{2,1,0:T(8,128)S(1)}, u32[]{:S(2)}, u32[]{:S(2)}) collective-permute-start(f32[16,64,128]{2,1,0:T(8,128)S(1)} %get-tuple-element.97), channel_id=1, source_target_pairs={{8,0},{16,8},{24,16},{32,24},{40,32},{48,40},{56,48},{64,56},{72,6... | collective-permute-start | bytes 1572872 | tf_op jit(solution)/shard_map/ppermute | solution.py:12
  228.9 0.7 copy-start.5
Sparse Core Ops, SparseCore 0:
  229.0 33.7 reduce-scatter.1
